TPU v7x, 32 devices: a whole 2x2x4 slice. The times are simulated.
32 devices in a mesh: patch: 8 (over z, y), band: 4 (over x, core).
Axes of the slice: x: 2, y: 2, z: 4, core: 2. Of those that a mesh axis runs over, the one named last changes fastest.
Arguments:
- exposures: float32 [64, 256, 128], P(('band', 'patch')), parts along dimension 0, may hold values from -6 to 6
- variance: float32 [64, 256, 128], P(('band', 'patch')), parts along dimension 0, may hold values from 0.01 to 60, as said below
- mask_bits: int32 [64, 256, 128], P(('band', 'patch')), parts along dimension 0, may hold values from 0 to 4095
- kernel_coeffs: float32 [64, 27, 6], P(('band', 'patch')), parts along dimension 0, may hold values from -3 to 3
- ccd_visit: int32 [64, 1], P(('band', 'patch')), parts along dimension 0, may hold values from 0 to 7
- strip_patch: int32 [2048, 1], P(('band', 'patch')), parts along dimension 0, may hold values from 0 to 7, as said below
- strip_row: int32 [2048], P(('band', 'patch')), parts along dimension 0, may hold values from 0 to 120
- strip_col: int32 [2048], P(('band', 'patch')), parts along dimension 0, may hold values from 0 to 384
Outputs:
- coadd_image: float32 [32, 128, 512], P(('band', 'patch')), parts along dimension 0
- weight_map: float32 [32, 128, 512], P(('band', 'patch')), parts along dimension 0
There are 4 independent parts, one for each index of `band`. A program takes and returns all parts, laid end to end along the dimension named above; each array names one. Nothing has to cross between parts.
Inputs may be any that keep to these rules, and one draw needn't show every extreme that they name: `variance`: Positive. `ccd_visit`: every visit has at least one CCD. `strip_patch`: among the strips of one device (aligned blocks of 64 rows) no patch is named more than 16 times; one patch is named exactly 16 times in every block.
All inputs are finite; a program needn't handle non-finite values.
Results may differ from a plain program's by a relative error of at most 0.00011.
Values sent between devices are 32-bit elements; how exact they have to be, the bound alone decides.
No kernel may reach another device: no remote copies, remote signals or barrier semaphores. Data moves between devices by JAX's collectives and lax.ppermute only.
A program may use at most 64 MiB of HBM per device.

v0:
```python
import math
import jax
import numpy as np
import jax.numpy as jnp
from jax import lax
from jax.sharding import PartitionSpec as P

PH = 128
PW = 512
KS = 21
VISITS = 8
gauss_widths = (0.75, 1.5, 3.0)
largest_value = lax.Precision.HIGHEST
mxu_value = lax.Precision.HIGH


def tap_table(kernel_half_width):
    support = np.arange(-kernel_half_width, kernel_half_width + 1).astype(np.float64)
    tables = []
    for spread in gauss_widths:
        s32 = float(np.float32(spread))
        gauss_total = np.sum(np.exp(-support * support / (2.0 * s32 * s32)))
        profile = np.exp(-support * support / (2.0 * s32 * s32)) / gauss_total
        scaled = support / s32
        tables.append(np.stack([profile, profile * scaled, profile * scaled * scaled]))
    return np.stack(tables)


def row_blocks(block_rows, window_rows, kernel_half_width):
    taps = tap_table(kernel_half_width).reshape(9, 2 * kernel_half_width + 1)
    out = np.zeros((9, block_rows, window_rows), np.float64)
    for i in range(block_rows):
        out[:, i, i : i + 2 * kernel_half_width + 1] = taps
    return out.astype(np.float32)


def column_ops(column_count, kernel_half_width):
    taps = tap_table(kernel_half_width)
    out = np.zeros((3, 3, column_count, column_count), np.float64)
    for y in range(column_count):
        lo = max(0, y - kernel_half_width)
        hi = min(column_count, y + kernel_half_width + 1)
        for x in range(lo, hi):
            out[:, :, y, x] = taps[:, :, y - x + kernel_half_width]
    return out.astype(np.float32)


def convolve_all(exposures, kernel_coeffs):
    kernel_half_width = KS // 2
    n, height, columns = exposures.shape
    block = 8
    blocks = height // block
    span = 2 * kernel_half_width + block
    reach = -(-span // block)
    total_rows = (blocks + reach - 1) * block
    padded = jnp.pad(
        exposures, ((0, 0), (kernel_half_width, total_rows - height - kernel_half_width), (0, 0))
    ).reshape(n, blocks + reach - 1, block, columns)
    windows = jnp.concatenate([padded[:, j : j + blocks] for j in range(reach)], axis=2)
    rows = jnp.asarray(row_blocks(block, reach * block, kernel_half_width))
    smooth = jnp.einsum("kit,nqtx->nqkix", rows, windows, precision=mxu_value)
    col_ops = jnp.asarray(column_ops(columns, kernel_half_width))
    x_line = 2.0 * jnp.arange(columns).astype(jnp.float32) / (columns - 1) - 1.0
    coef = kernel_coeffs.reshape(n, 3, 3, 3, 6)
    c = [coef[..., p, None] for p in range(6)]
    fx = jnp.stack(
        [
            c[0] + c[1] * x_line + c[3] * (x_line * x_line),
            c[2] + c[4] * x_line,
            jnp.broadcast_to(c[5], c[0].shape[:-1] + (columns,)),
        ],
        axis=4,
    )
    mixed = jnp.sum(col_ops[None, :, None, :, :, None, :] * fx[:, :, :, :, None, :, :], axis=3)
    mixed = mixed.reshape(n, 9, columns, 3 * columns)
    fields = jnp.einsum("nqkiy,nkyz->nqiz", smooth, mixed, precision=mxu_value)
    fields = fields.reshape(n, height, 3 * columns)
    y_line = (2.0 * jnp.arange(height).astype(jnp.float32) / (height - 1) - 1.0)[None, :, None]
    return (
        fields[:, :, :columns]
        + y_line * fields[:, :, columns : 2 * columns]
        + y_line * y_line * fields[:, :, 2 * columns :]
    )


def place_slots(flux_flat, weight_flat, offsets, patch_rows, patch_cols):
    slot_total, strip_rows, columns = flux_flat.shape
    group = math.gcd(slot_total, 16)
    pairs = jnp.stack([flux_flat, weight_flat], axis=1).reshape(
        slot_total // group, group, 2, strip_rows, columns
    )
    grouped_offsets = offsets.reshape(slot_total // group, group, offsets.shape[1])
    target_cols = jnp.arange(patch_cols)
    source_cols = jnp.arange(columns)
    target_rows = jnp.arange(patch_rows)
    source_rows = jnp.arange(strip_rows)

    def place_group(total, item):
        pixel_block_tile, block_offsets = item
        column_selection = (
            target_cols[None, None, :]
            == block_offsets[:, 1][:, None, None] + source_cols[None, :, None]
        ).astype(jnp.float32)
        row_select = (
            target_rows[None, :, None]
            == block_offsets[:, 0][:, None, None] + source_rows[None, None, :]
        ).astype(jnp.float32)
        broadened_width = jnp.einsum(
            "vmwn,vny->vmwy", pixel_block_tile, column_selection, precision=largest_value
        )
        return (
            total
            + jnp.einsum("gri,gkip->krp", row_select, broadened_width, precision=largest_value),
            None,
        )

    start = jnp.zeros((2, patch_rows, patch_cols), jnp.float32)
    placed, _ = lax.scan(place_group, start, (pairs, grouped_offsets))
    return (placed[0], placed[1])


def shards(
    exposures, variance, mask_bits, kernel_coeffs, ccd_visit, strip_patch, strip_row, strip_col
):
    ccd_count, height, columns = exposures.shape
    strip_total = strip_patch.shape[0]
    per_ccd = strip_total // ccd_count
    strip_rows = height // per_ccd
    devices = lax.axis_size("patch")
    capacity = 2 * strip_total // devices
    usable = (jnp.bitwise_and(mask_bits, 3) != 3).astype(jnp.float32)
    visit_hot = (ccd_visit == jnp.arange(VISITS)[None, :]).astype(jnp.float32)
    local_count = jnp.sum(jnp.sum(usable, axis=(1, 2))[:, None] * visit_hot, axis=0)
    local_load = jnp.sum(jnp.sum(usable * variance, axis=(1, 2))[:, None] * visit_hot, axis=0)
    destination = strip_patch[:, 0]
    strip_ids = jnp.arange(strip_total)
    earlier = strip_ids[None, :] < strip_ids[:, None]
    same_target = destination[None, :] == destination[:, None]
    slot_rank = jnp.sum(jnp.logical_and(earlier, same_target).astype(jnp.int32), axis=1)
    slot_index = destination * capacity + slot_rank
    slot_total = devices * capacity
    chooser = (slot_index[None, :] == jnp.arange(slot_total)[:, None]).astype(jnp.float32)
    strip_visit = jnp.repeat(ccd_visit[:, 0], per_ccd)
    placement = jnp.stack([strip_row, strip_col, strip_visit], axis=1).astype(jnp.float32)
    slot_meta = jnp.dot(chooser, placement, precision=largest_value).reshape(devices, capacity, 3)
    meta = jnp.zeros((devices, 8, columns), jnp.float32)
    meta = meta.at[:, 0:3, :capacity].set(jnp.swapaxes(slot_meta, 1, 2))
    meta = meta.at[:, 3, :VISITS].set(jnp.broadcast_to(local_count, (devices, VISITS)))
    meta = meta.at[:, 4, :VISITS].set(jnp.broadcast_to(local_load, (devices, VISITS)))
    body_rows = capacity * strip_rows
    weight_tiles = usable.reshape(strip_total, strip_rows * columns)
    weight_packed = jnp.dot(chooser, weight_tiles, precision=largest_value).reshape(
        devices, body_rows, columns
    )
    first = jnp.concatenate([weight_packed, meta], axis=1)
    got_first = lax.all_to_all(first, "patch", split_axis=0, concat_axis=0, tiled=True)
    convolved = convolve_all(exposures, kernel_coeffs)
    flux_tiles = (usable * convolved).reshape(strip_total, strip_rows * columns)
    flux_packed = jnp.dot(chooser, flux_tiles, precision=largest_value).reshape(
        devices, body_rows, columns
    )
    got_flux = lax.all_to_all(flux_packed, "patch", split_axis=0, concat_axis=0, tiled=True)
    got_meta = got_first[:, body_rows:, :]
    visit_count = jnp.sum(got_meta[:, 3, :VISITS], axis=0)
    visit_load = jnp.sum(got_meta[:, 4, :VISITS], axis=0)
    visit_weight = (visit_count + 1.0) / (visit_load + 1.0)
    slot_rows = got_meta[:, 0, :capacity].reshape(slot_total).astype(jnp.int32)
    slot_cols = got_meta[:, 1, :capacity].reshape(slot_total).astype(jnp.int32)
    slot_visit = got_meta[:, 2, :capacity].reshape(slot_total).astype(jnp.int32)
    slot_hot = (slot_visit[:, None] == jnp.arange(VISITS)[None, :]).astype(jnp.float32)
    slot_weight = jnp.sum(slot_hot * visit_weight[None, :], axis=1)
    weight_body = got_first[:, :body_rows, :].reshape(slot_total, strip_rows, columns)
    flux_body = got_flux.reshape(slot_total, strip_rows, columns)
    weight_body = weight_body * slot_weight[:, None, None]
    flux_body = flux_body * slot_weight[:, None, None]
    offsets = jnp.stack([slot_rows, slot_cols], axis=1)
    numerator, weight_map = place_slots(flux_body, weight_body, offsets, PH, PW)
    coadd_image = numerator / jnp.maximum(weight_map, 1.0)
    return (coadd_image[None], weight_map[None])


def solution(mesh):
    return jax.shard_map(
        shards,
        mesh=mesh,
        in_specs=(
            P(("band", "patch"), None, None),
            P(("band", "patch"), None, None),
            P(("band", "patch"), None, None),
            P(("band", "patch"), None, None),
            P(("band", "patch"), None),
            P(("band", "patch"), None),
            P(("band", "patch")),
            P(("band", "patch")),
        ),
        out_specs=(P(("band", "patch"), None, None), P(("band", "patch"), None, None)),
        check_vma=False,
    )
```

profile of v0, /device:TPU:0, one launch (start us, length us, event | category | flops | bytes accessed | tf_op | source)
XLA Modules:
  0.0 81.9 jit_solution(7379162448762953336)
XLA Ops:
  0.7 0.8 copy.70
  1.4 0.2 fusion.51
  1.7 0.2 copy.71
  1.9 0.2 copy.73
  2.1 0.2 copy.75
  2.3 0.2 copy.77
  2.6 0.2 copy.79
  2.8 0.2 copy.81
  3.0 0.4 multiply_add_fusion.1
  3.4 0.1 stack_broadcast_in_dim.2
  3.5 0.1 pad_maximum_fusion.2
  3.6 4.2 %multiply_reduce_fusion = f32[2,3,3,128,3,128]{5,3,4,2,1,0:T(8,128)} fusion(f32[2,3,3,3,3,128]{5,4,3,2,1,0:T(4,128)S(1)} %pad_maximum_fusion.2, f32[3,3,128,128]{3,2,1,0:T(8,128)} %constant.143.clone), kind=kLoop, calls=%fused_computation.20 | loop fusion | flops 4423680 | bytes 4211712 | tf_op jit(solution)/shard_map/reduce_sum | solution.py:74
  7.8 3.3 %copy.83 = f32[2,3,3,128,3,128]{3,5,4,2,1,0:T(8,128)S(1)} copy(f32[2,3,3,128,3,128]{5,3,4,2,1,0:T(8,128)} %multiply_reduce_fusion) | data formatting | bytes 7077888 | tf_op jit(solution)/shard_map/reduce_sum | solution.py:74
  11.1 1.0 %pad_bitcast_fusion = f32[2,35,8,128]{3,2,1,0:T(8,128)S(1)} fusion(f32[2,256,128]{2,1,0:T(8,128)} %param.18), kind=kLoop, calls=%fused_computation.37 | loop fusion | bytes 548864 | tf_op jit(solution)/shard_map/reshape | solution.py:58
  12.1 1.8 %fusion.22 = f32[2,32,128,9,8]{2,4,3,1,0:T(8,128)S(1)} fusion(f32[9,8,32,1,1]{2,1,0,4,3:T(8,128)} %constant.153, f32[2,32,8,128]{3,2,1,0:T(8,128)S(1)} %get-tuple-element.177, f32[2,32,8,128]{3,2,1,0:T(8,128)S(1)} %get-tuple-element.178, f32[2,32,8,128]{3,2,1,0:T(8,128)S(1)} %get-tuple-element.179, f32[2,32,8,128]{3,2,1,0:T(8,128)S(1)} %get-tuple-element.176), kind=kOutput, calls=%fused_computation.25 | convolution fusion | flops 114032640 | bytes 3417088 | tf_op jit(solution)/shard_map/kit,nqtx->nqkix/dot_general | solution.py:61
  14.0 2.3 %fusion.19 = f32[2,256,384]{2,1,0:T(8,128)S(1)} fusion(f32[2,9,128,384,1]{2,3,1,4,0:T(8,128)S(1)} %bitcast.101, f32[2,32,128,9,8]{2,4,3,1,0:T(8,128)S(1)} %fusion.22), kind=kOutput, calls=%fused_computation.23 | convolution fusion | flops 1358954496 | bytes 6684672 | tf_op jit(solution)/shard_map/nqkiy,nkyz->nqiz/dot_general | solution.py:76
  16.3 0.1 fusion.31
  16.4 0.1 reshape.331
  16.5 1.1 %select_reduce_fusion = (f32[2]{0:T(128)S(1)}, f32[2]{0:T(128)S(1)}) fusion(pred[2,256,128]{2,1,0:T(32,128)(4,1)S(1)} %get-tuple-element.171, f32[2,256,128]{2,1,0:T(8,128)} %param.19), kind=kLoop, calls=%fused_computation.44 | loop fusion | flops 262140 | bytes 327696 | tf_op jit(solution)/shard_map/reduce_sum | solution.py:134
  17.6 0.2 convert_reduce_fusion.1
  17.9 0.1 stack_reshape.3
  18.0 0.8 fusion.33
  18.8 0.1 reshape.333
  18.9 0.2 fusion.34
  19.2 0.1 reshape.332
  19.3 0.1 select_reduce_fusion.2
  19.4 0.3 scatter.11
  19.7 0.3 scatter.14
  19.9 0.8 %pad_maximum_fusion.1 = f32[8,136,128]{2,1,0:T(8,128)} fusion(f32[8,8,128]{2,1,0:T(8,128)S(1)} %scatter.14, f32[8,128,128]{2,1,0:T(8,128)S(1)} %reshape.332), kind=kLoop, calls=%fused_computation.33 | loop fusion | flops 139264 | bytes 1114112 | tf_op jit(solution)/shard_map/concatenate | solution.py:155
  20.8 7.3 %all-to-all-start.1 = ((f32[8,136,128]{2,1,0:T(8,128)}), f32[8,136,128]{2,1,0:T(8,128)S(1)}, u32[]{:S(2)}, u32[]{:S(2)}) async-start(f32[8,136,128]{2,1,0:T(8,128)} %pad_maximum_fusion.1), calls=%async_computation.1 | async-start | bytes 1114112 | tf_op jit(solution)/shard_map/all_to_all | solution.py:156
  28.1 0.4 fusion.35
  28.5 0.9 %reshape.329 = f32[8,128,128]{2,1,0:T(8,128)} reshape(f32[128,1024]{1,0:T(8,128)S(1)} %fusion.35) | data formatting | bytes 1048576 | tf_op jit(solution)/shard_map/reshape | solution.py:159
  29.4 13.9 %all-to-all-done.1 = f32[8,136,128]{2,1,0:T(8,128)S(1)} async-done(((f32[8,136,128]{2,1,0:T(8,128)}), f32[8,136,128]{2,1,0:T(8,128)S(1)}, u32[]{:S(2)}, u32[]{:S(2)}) %all-to-all-start.1) | async-done | bytes 557088 | tf_op jit(solution)/shard_map/all_to_all | solution.py:156
  43.3 3.6 %all-to-all-start = ((f32[8,128,128]{2,1,0:T(8,128)}), f32[8,128,128]{2,1,0:T(8,128)S(1)}, u32[]{:S(2)}, u32[]{:S(2)}) async-start(f32[8,128,128]{2,1,0:T(8,128)} %reshape.329), calls=%async_computation | async-start | bytes 1048576 | tf_op jit(solution)/shard_map/all_to_all | solution.py:162
  47.0 0.1 convert_element_type.88
  47.0 0.1 select_reduce_fusion.1
  47.1 0.1 mul.218
  47.3 14.3 %all-to-all-done = f32[8,128,128]{2,1,0:T(8,128)S(1)} async-done(((f32[8,128,128]{2,1,0:T(8,128)}), f32[8,128,128]{2,1,0:T(8,128)S(1)}, u32[]{:S(2)}, u32[]{:S(2)}) %all-to-all-start) | async-done | bytes 524320 | tf_op jit(solution)/shard_map/all_to_all | solution.py:162
  61.6 0.2 bitcast_multiply_fusion
  61.9 19.0 %while.16 = (s32[]{:T(128)}, f32[2,128,512]{1,2,0:T(8,128)S(1)}, f32[8,16,2,8,128]{4,3,2,1,0:T(8,128)S(1)}, s32[8,16,2]{1,0,2:T(8,128)S(1)}, s32[]{:T(128)}, /*index=5*/s32[]{:T(128)}) while((s32[]{:T(128)}, f32[2,128,512]{1,2,0:T(8,128)S(1)}, f32[8,16,2,8,128]{4,3,2,1,0:T(8,128)S(1)}, s32[8,16,2]{1,0,2:T(8,128)S(1)}, ...), condition=%wide.region_10.11_spmd.clone.clone, body=%wide.region_9.10_spmd.clone.clone.sunk | while | flops 403982464 | bytes 2246359 | solution.py:118
  61.9 0.1 iota_add_fusion.4
  62.0 1.5 %fusion.67 = f32[16,2,8,512]{3,2,1,0:T(8,128)S(1)} fusion(s32[16,128]{1,0:T(8,128)S(1)} %iota_add_fusion.4, f32[8,16,2,8,128]{4,3,2,1,0:T(8,128)S(1)} %get-tuple-element.237, s32[]{:T(128)} %get-tuple-element.229), kind=kOutput, calls=%fused_computation.5.clone.1 | convolution fusion | flops 202375168 | bytes 663556 | tf_op jit(solution)/shard_map/while/body/eval_jaxpr/vmwn,vny->vmwy/dot_general | solution.py:108
  63.5 0.7 fusion.68
  64.3 0.1 iota_add_fusion.4
  64.3 1.5 %fusion.67 = f32[16,2,8,512]{3,2,1,0:T(8,128)S(1)} fusion(s32[16,128]{1,0:T(8,128)S(1)} %iota_add_fusion.4, f32[8,16,2,8,128]{4,3,2,1,0:T(8,128)S(1)} %get-tuple-element.237, s32[]{:T(128)} %get-tuple-element.229), kind=kOutput, calls=%fused_computation.5.clone.1 | convolution fusion | flops 202375168 | bytes 663556 | tf_op jit(solution)/shard_map/while/body/eval_jaxpr/vmwn,vny->vmwy/dot_general | solution.py:108
  65.9 0.7 fusion.68
  66.6 0.1 iota_add_fusion.4
  66.7 1.5 %fusion.67 = f32[16,2,8,512]{3,2,1,0:T(8,128)S(1)} fusion(s32[16,128]{1,0:T(8,128)S(1)} %iota_add_fusion.4, f32[8,16,2,8,128]{4,3,2,1,0:T(8,128)S(1)} %get-tuple-element.237, s32[]{:T(128)} %get-tuple-element.229), kind=kOutput, calls=%fused_computation.5.clone.1 | convolution fusion | flops 202375168 | bytes 663556 | tf_op jit(solution)/shard_map/while/body/eval_jaxpr/vmwn,vny->vmwy/dot_general | solution.py:108
  68.3 0.7 fusion.68
  69.0 0.1 iota_add_fusion.4
  69.1 1.5 %fusion.67 = f32[16,2,8,512]{3,2,1,0:T(8,128)S(1)} fusion(s32[16,128]{1,0:T(8,128)S(1)} %iota_add_fusion.4, f32[8,16,2,8,128]{4,3,2,1,0:T(8,128)S(1)} %get-tuple-element.237, s32[]{:T(128)} %get-tuple-element.229), kind=kOutput, calls=%fused_computation.5.clone.1 | convolution fusion | flops 202375168 | bytes 663556 | tf_op jit(solution)/shard_map/while/body/eval_jaxpr/vmwn,vny->vmwy/dot_general | solution.py:108
  70.6 0.7 fusion.68
  71.4 0.1 iota_add_fusion.4
  71.5 1.5 %fusion.67 = f32[16,2,8,512]{3,2,1,0:T(8,128)S(1)} fusion(s32[16,128]{1,0:T(8,128)S(1)} %iota_add_fusion.4, f32[8,16,2,8,128]{4,3,2,1,0:T(8,128)S(1)} %get-tuple-element.237, s32[]{:T(128)} %get-tuple-element.229), kind=kOutput, calls=%fused_computation.5.clone.1 | convolution fusion | flops 202375168 | bytes 663556 | tf_op jit(solution)/shard_map/while/body/eval_jaxpr/vmwn,vny->vmwy/dot_general | solution.py:108
  73.0 0.7 fusion.68
  73.8 0.1 iota_add_fusion.4
  73.8 1.5 %fusion.67 = f32[16,2,8,512]{3,2,1,0:T(8,128)S(1)} fusion(s32[16,128]{1,0:T(8,128)S(1)} %iota_add_fusion.4, f32[8,16,2,8,128]{4,3,2,1,0:T(8,128)S(1)} %get-tuple-element.237, s32[]{:T(128)} %get-tuple-element.229), kind=kOutput, calls=%fused_computation.5.clone.1 | convolution fusion | flops 202375168 | bytes 663556 | tf_op jit(solution)/shard_map/while/body/eval_jaxpr/vmwn,vny->vmwy/dot_general | solution.py:108
  75.4 0.7 fusion.68
  76.2 1.5 %fusion.67 = f32[16,2,8,512]{3,2,1,0:T(8,128)S(1)} fusion(s32[16,128]{1,0:T(8,128)S(1)} %iota_add_fusion.4, f32[8,16,2,8,128]{4,3,2,1,0:T(8,128)S(1)} %get-tuple-element.237, s32[]{:T(128)} %get-tuple-element.229), kind=kOutput, calls=%fused_computation.5.clone.1 | convolution fusion | flops 202375168 | bytes 663556 | tf_op jit(solution)/shard_map/while/body/eval_jaxpr/vmwn,vny->vmwy/dot_general | solution.py:108
  77.7 0.7 fusion.68
  78.6 1.5 %fusion.67 = f32[16,2,8,512]{3,2,1,0:T(8,128)S(1)} fusion(s32[16,128]{1,0:T(8,128)S(1)} %iota_add_fusion.4, f32[8,16,2,8,128]{4,3,2,1,0:T(8,128)S(1)} %get-tuple-element.237, s32[]{:T(128)} %get-tuple-element.229), kind=kOutput, calls=%fused_computation.5.clone.1 | convolution fusion | flops 202375168 | bytes 663556 | tf_op jit(solution)/shard_map/while/body/eval_jaxpr/vmwn,vny->vmwy/dot_general | solution.py:108
  80.1 0.7 fusion.68
  80.9 0.2 copy.90
  81.1 0.8 slice_divide_fusion
  (57 shorter events, 1.2 us)
Async XLA Ops:
  14.0 2.3 %copy-start = (s32[2,256,128]{2,1,0:T(8,128)S(1)}, s32[2,256,128]{2,1,0:T(8,128)}, u32[]{:S(2)}) copy-start(s32[2,256,128]{2,1,0:T(8,128)} %param.20) | copy-start | bytes 786436
  14.0 3.7 %copy-start.2 = (s32[64,1]{0,1:T(1,128)S(1)}, s32[64,1]{0,1:T(1,128)}, u32[]{:S(2)}) copy-start(s32[64,1]{0,1:T(1,128)} %param.23) | copy-start | bytes 772
  14.0 3.8 %copy-start.1 = (s32[2,1]{0,1:T(1,128)S(1)}, s32[2,1]{0,1:T(1,128)}, u32[]{:S(2)}) copy-start(s32[2,1]{0,1:T(1,128)} %param.22) | copy-start | bytes 28
  20.8 22.5 %all-to-all-start.1 = ((f32[8,136,128]{2,1,0:T(8,128)}), f32[8,136,128]{2,1,0:T(8,128)S(1)}, u32[]{:S(2)}, u32[]{:S(2)}) async-start(f32[8,136,128]{2,1,0:T(8,128)} %pad_maximum_fusion.1), calls=%async_computation.1 | async-start | bytes 1114112 | tf_op jit(solution)/shard_map/all_to_all | solution.py:156
  43.3 18.3 %all-to-all-start = ((f32[8,128,128]{2,1,0:T(8,128)}), f32[8,128,128]{2,1,0:T(8,128)S(1)}, u32[]{:S(2)}, u32[]{:S(2)}) async-start(f32[8,128,128]{2,1,0:T(8,128)} %reshape.329), calls=%async_computation | async-start | bytes 1048576 | tf_op jit(solution)/shard_map/all_to_all | solution.py:162
where the time goes:
time: 82.4 us; the launch traced here: 81.9 us
  waiting for transfers between devices  28.2 us (34%)
  matrix products  22.9 us (28%)
  starting transfers between devices  10.9 us (13%)
  other arithmetic  9.37 us (11%)
  local copies, waits for them, and re-layouts  9.19 us (11%)
  between operations  0.95 us (1%)
    all_to_all x1, waiting for transfers between devices, shards(): lax.all_to_all(flux_packed, 'patch', split_axis=0, concat_axis=0, tiled=T...  14.3 us
    all_to_all x1, waiting for transfers between devices, shards(): lax.all_to_all(first, 'patch', split_axis=0, concat_axis=0, tiled=True)  13.9 us
    dot_general x8, matrix products, place_group(): jnp.einsum('vmwn,vny->vmwy', pixel_block_tile, column_selection, precisio...  11.7 us
    all_to_all x1, starting transfers between devices, shards(): lax.all_to_all(first, 'patch', split_axis=0, concat_axis=0, tiled=True)  7.31 us
    dot_general x8, matrix products, place_group(): jnp.einsum('gri,gkip->krp', row_select, broadened_width, precision=larges...  5.76 us
    reduce_sum x1, other arithmetic, convolve_all(): jnp.sum(col_ops[None, :, None, :, :, None, :] * fx[:, :, :, :, None, :, :...  4.17 us
    all_to_all x1, starting transfers between devices, shards(): lax.all_to_all(flux_packed, 'patch', split_axis=0, concat_axis=0, tiled=T...  3.64 us
    reduce_sum x1, local copies, waits for them, and re-layouts, convolve_all(): jnp.sum(col_ops[None, :, None, :, :, None, :] * fx[:, :, :, :, None, :, :...  3.31 us
  transfers between devices with their start and end apart: 2, of which 2 were waited for; matrix products, arithmetic and copies ran while one was open for 2% of the time, Pallas kernels for 0%

commit v1 on v0

--- a/solution.py
+++ b/solution.py
@@ -12,6 +12,19 @@
 gauss_widths = (0.75, 1.5, 3.0)
 largest_value = lax.Precision.HIGHEST
 mxu_value = lax.Precision.HIGH
+
+
+def edges_load(chunk, out_dim, unit):
+    fresh, block_next = (chunk.shape[:out_dim], chunk.shape[out_dim + 1 :])
+    h_now = jnp.moveaxis(chunk.reshape(*fresh, unit, -1, *block_next), out_dim, 0)
+    return h_now
+
+
+def perform_inputs(state, dim_at):
+    spare = list(state.shape[1:])
+    spare[dim_at] *= state.shape[0]
+    left_arr = jnp.moveaxis(state, 0, dim_at).reshape(spare)
+    return left_arr
 
 
 def tap_table(kernel_half_width):
@@ -153,7 +166,16 @@
         devices, body_rows, columns
     )
     first = jnp.concatenate([weight_packed, meta], axis=1)
-    got_first = lax.all_to_all(first, "patch", split_axis=0, concat_axis=0, tiled=True)
+    r1, met_up = (lax.axis_size("patch"), lax.axis_index("patch"))
+    clean = edges_load(first, 0, r1)
+    so_far_all = [clean[met_up]]
+    for q in tuple(range(1, r1)):
+        reply = clean[(met_up + q) % r1]
+        so_far_all.append(
+            lax.ppermute(reply, axis_name="patch", perm=[(it, (it + q) % r1) for it in range(r1)])
+        )
+    clean = jnp.stack(so_far_all)[(met_up - jnp.arange(r1)) % r1]
+    got_first = perform_inputs(clean, 0)
     convolved = convolve_all(exposures, kernel_coeffs)
     flux_tiles = (usable * convolved).reshape(strip_total, strip_rows * columns)
     flux_packed = jnp.dot(chooser, flux_tiles, precision=largest_value).reshape(

time: 82.4 us -> 74.3 us (0.902)
  waiting for transfers between devices: 28.2 us -> 9.59 us
  starting transfers between devices: 10.9 us -> 21 us
    ppermute x0 -> x7, starting transfers between devices: none -> 16 us  [shards(): lax.ppermute(reply, axis_name='patch', perm=[(it, (it + q) % r1) for it i...]
    all_to_all x1 -> x0, waiting for transfers between devices: 13.9 us -> none  [shards(): lax.all_to_all(first, 'patch', split_axis=0, concat_axis=0, tiled=True)]
    all_to_all x1, waiting for transfers between devices: 14.3 us -> 4.96 us  [shards(): lax.all_to_all(flux_packed, 'patch', split_axis=0, concat_axis=0, tiled=T...]
    all_to_all x1 -> x0, starting transfers between devices: 7.31 us -> none  [shards(): lax.all_to_all(first, 'patch', split_axis=0, concat_axis=0, tiled=True)]
    ppermute x0 -> x7, waiting for transfers between devices: none -> 4.63 us  [shards(): lax.ppermute(reply, axis_name='patch', perm=[(it, (it + q) % r1) for it i...]
    all_to_all x1, starting transfers between devices: 3.64 us -> 5.03 us  [shards(): lax.all_to_all(flux_packed, 'patch', split_axis=0, concat_axis=0, tiled=T...]
  transfers between devices with their start and end apart: 2 -> 8, of which waited for: 2 -> 3; matrix products, arithmetic and copies ran while one was open for 2% -> 3% of each run, Pallas kernels for 0% -> 0%
where the time goes in v1:
time: 74.3 us; the launch traced here: 73.6 us
  matrix products  22.9 us (31%)
  starting transfers between devices  21 us (28%)
  local copies, waits for them, and re-layouts  9.81 us (13%)
  waiting for transfers between devices  9.59 us (13%)
  other arithmetic  8.82 us (12%)
  between operations  1.06 us (1%)
    ppermute x7, starting transfers between devices, shards(): lax.ppermute(reply, axis_name='patch', perm=[(it, (it + q) % r1) for it i...  16 us
    dot_general x8, matrix products, place_group(): jnp.einsum('vmwn,vny->vmwy', pixel_block_tile, column_selection, precisio...  11.7 us
    dot_general x8, matrix products, place_group(): jnp.einsum('gri,gkip->krp', row_select, broadened_width, precision=larges...  5.73 us
    all_to_all x1, starting transfers between devices, shards(): lax.all_to_all(flux_packed, 'patch', split_axis=0, concat_axis=0, tiled=T...  5.03 us
    all_to_all x1, waiting for transfers between devices, shards(): lax.all_to_all(flux_packed, 'patch', split_axis=0, concat_axis=0, tiled=T...  4.96 us
    ppermute x7, waiting for transfers between devices, shards(): lax.ppermute(reply, axis_name='patch', perm=[(it, (it + q) % r1) for it i...  4.63 us
    reduce_sum x1, other arithmetic, convolve_all(): jnp.sum(col_ops[None, :, None, :, :, None, :] * fx[:, :, :, :, None, :, :...  4.17 us
    reduce_sum x1, local copies, waits for them, and re-layouts, convolve_all(): jnp.sum(col_ops[None, :, None, :, :, None, :] * fx[:, :, :, :, None, :, :...  3.31 us
  transfers between devices with their start and end apart: 8, of which 3 were waited for; matrix products, arithmetic and copies ran while one was open for 3% of the time, Pallas kernels for 0%

profile of v1, /device:TPU:0, one launch (start us, length us, event | category | flops | bytes accessed | tf_op | source)
XLA Modules:
  0.0 73.6 jit_solution(8494723108381939552)
XLA Ops:
  0.7 0.8 %copy.55 = f32[2,27,6]{2,0,1:T(2,128)S(1)} copy(f32[2,27,6]{1,0,2:T(2,128)} %param.21) | data formatting | bytes 2592 | tf_op args[3]
  1.5 0.2 fusion.60
  1.7 0.2 copy.56
  1.9 0.2 copy.58
  2.1 0.2 copy.60
  2.4 0.2 copy.62
  2.6 0.2 copy.64
  2.8 0.2 copy.66
  3.0 0.4 multiply_add_fusion.1
  3.4 0.1 stack_broadcast_in_dim.2
  3.6 4.2 %multiply_reduce_fusion = f32[2,3,3,128,3,128]{5,3,4,2,1,0:T(8,128)} fusion(f32[2,3,3,3,3,128]{5,4,3,2,1,0:T(4,128)S(1)} %pad_maximum_fusion.1, f32[3,3,128,128]{3,2,1,0:T(8,128)} %constant.206.clone), kind=kLoop, calls=%fused_computation.21 | loop fusion | flops 4423680 | bytes 4211712 | tf_op jit(solution)/shard_map/reduce_sum | solution.py:87
  7.8 3.3 %copy.68 = f32[2,3,3,128,3,128]{3,5,4,2,1,0:T(8,128)S(1)} copy(f32[2,3,3,128,3,128]{5,3,4,2,1,0:T(8,128)} %multiply_reduce_fusion) | data formatting | bytes 7077888 | tf_op jit(solution)/shard_map/reduce_sum | solution.py:87
  11.1 1.0 %pad_bitcast_fusion = f32[2,35,8,128]{3,2,1,0:T(8,128)S(1)} fusion(f32[2,256,128]{2,1,0:T(8,128)} %param.18), kind=kLoop, calls=%fused_computation.53 | loop fusion | bytes 548864 | tf_op jit(solution)/shard_map/reshape | solution.py:71
  12.1 1.8 %fusion.21 = f32[2,32,128,9,8]{2,4,3,1,0:T(8,128)S(1)} fusion(f32[9,8,32,1,1]{2,1,0,4,3:T(8,128)} %constant.216, f32[2,32,8,128]{3,2,1,0:T(8,128)S(1)} %get-tuple-element.179, f32[2,32,8,128]{3,2,1,0:T(8,128)S(1)} %get-tuple-element.180, f32[2,32,8,128]{3,2,1,0:T(8,128)S(1)} %get-tuple-element.181, f32[2,32,8,128]{3,2,1,0:T(8,128)S(1)} %get-tuple-element.178), kind=kOutput, calls=%fused_computation.34 | convolution fusion | flops 114032640 | bytes 3417088 | tf_op jit(solution)/shard_map/kit,nqtx->nqkix/dot_general | solution.py:74
  14.0 2.3 %fusion.18 = f32[2,256,384]{2,1,0:T(8,128)S(1)} fusion(f32[2,9,128,384,1]{2,3,1,4,0:T(8,128)S(1)} %bitcast.127, f32[2,32,128,9,8]{2,4,3,1,0:T(8,128)S(1)} %fusion.21), kind=kOutput, calls=%fused_computation.32 | convolution fusion | flops 1358954496 | bytes 6684672 | tf_op jit(solution)/shard_map/nqkiy,nkyz->nqiz/dot_general | solution.py:89
  16.3 0.1 fusion.30
  16.5 1.1 %select_reduce_fusion = (f32[2]{0:T(128)S(1)}, f32[2]{0:T(128)S(1)}) fusion(pred[2,256,128]{2,1,0:T(32,128)(4,1)S(1)} %get-tuple-element.167, f32[2,256,128]{2,1,0:T(8,128)} %param.19), kind=kLoop, calls=%fused_computation.60 | loop fusion | flops 262140 | bytes 327696 | tf_op jit(solution)/shard_map/reduce_sum | solution.py:147
  17.7 0.2 convert_reduce_fusion.1
  18.0 0.8 %fusion.42 = f32[128,3]{0,1:T(4,128)S(1)} fusion(s32[64]{0:T(128)S(1)} %multiply_add_fusion.4, s32[64,1]{0,1:T(1,128)S(1)} %stack_reshape.3, s32[64,1]{0,1:T(1,128)} %bitcast.143, s32[64,1]{0,1:T(1,128)} %bitcast.144), kind=kOutput, calls=%fused_computation.82 | convolution fusion | flops 303680 | bytes 2560 | tf_op jit(solution)/shard_map/dot_general | solution.py:158
  18.8 0.1 reshape.401
  19.0 0.2 fusion.43
  19.4 0.3 scatter.11
  19.7 0.3 scatter.14
  20.0 5.1 %collective-permute-start.5 = (f32[1,136,128]{2,1,0:T(8,128)S(1)}, f32[1,136,128]{2,1,0:T(8,128)S(1)}, u32[]{:S(2)}, u32[]{:S(2)}) collective-permute-start(f32[1,136,128]{2,1,0:T(8,128)S(1)} %fusion.41), channel_id=1, source_target_pairs={{0,24},{4,28},{8,0},{12,4},{16,8},{20,12},{24,16},{28,20},{1,25},{... | collective-permute-start | bytes 208904 | tf_op jit(solution)/shard_map/ppermute | solution.py:175
  25.1 1.6 %collective-permute-start = (f32[1,136,128]{2,1,0:T(8,128)S(1)}, f32[1,136,128]{2,1,0:T(8,128)S(1)}, u32[]{:S(2)}, u32[]{:S(2)}) collective-permute-start(f32[1,136,128]{2,1,0:T(8,128)S(1)} %get-tuple-element.173), channel_id=1, source_target_pairs={{0,4},{4,8},{8,12},{12,16},{16,20},{20,24},{24,28},{28,0},{1,5},{5... | collective-permute-start | bytes 208904 | tf_op jit(solution)/shard_map/ppermute | solution.py:175
  26.7 1.0 %collective-permute-start.2 = (f32[1,136,128]{2,1,0:T(8,128)S(1)}, f32[1,136,128]{2,1,0:T(8,128)S(1)}, u32[]{:S(2)}, u32[]{:S(2)}) collective-permute-start(f32[1,136,128]{2,1,0:T(8,128)S(1)} %get-tuple-element.175), channel_id=1, source_target_pairs={{0,12},{4,16},{8,20},{12,24},{16,28},{20,0},{24,4},{28,8},{1,13},{... | collective-permute-start | bytes 208904 | tf_op jit(solution)/shard_map/ppermute | solution.py:175
  27.7 2.9 %collective-permute-start.3 = (f32[1,136,128]{2,1,0:T(8,128)S(1)}, f32[1,136,128]{2,1,0:T(8,128)S(1)}, u32[]{:S(2)}, u32[]{:S(2)}) collective-permute-start(f32[1,136,128]{2,1,0:T(8,128)S(1)} %get-tuple-element.176), channel_id=1, source_target_pairs={{0,16},{4,20},{8,24},{12,28},{16,0},{20,4},{24,8},{28,12},{1,17},{... | collective-permute-start | bytes 208904 | tf_op jit(solution)/shard_map/ppermute | solution.py:175
  30.7 0.4 fusion.44
  31.0 0.9 %reshape.397 = f32[8,128,128]{2,1,0:T(8,128)} reshape(f32[128,1024]{1,0:T(8,128)S(1)} %fusion.44) | data formatting | bytes 1048576 | tf_op jit(solution)/shard_map/reshape | solution.py:181
  31.9 5.0 %all-to-all-start = ((f32[8,128,128]{2,1,0:T(8,128)}), f32[8,128,128]{2,1,0:T(8,128)S(1)}, u32[]{:S(2)}, u32[]{:S(2)}) async-start(f32[8,128,128]{2,1,0:T(8,128)} %reshape.397), calls=%async_computation | async-start | bytes 1048576 | tf_op jit(solution)/shard_map/all_to_all | solution.py:184
  37.0 3.9 %collective-permute-start.4 = (f32[1,136,128]{2,1,0:T(8,128)S(1)}, f32[1,136,128]{2,1,0:T(8,128)S(1)}, u32[]{:S(2)}, u32[]{:S(2)}) collective-permute-start(f32[1,136,128]{2,1,0:T(8,128)S(1)} %get-tuple-element.177), channel_id=1, source_target_pairs={{0,20},{4,24},{8,28},{12,0},{16,4},{20,8},{24,12},{28,16},{1,21},{... | collective-permute-start | bytes 208904 | tf_op jit(solution)/shard_map/ppermute | solution.py:175
  40.9 1.5 %collective-permute-start.6 = (f32[1,136,128]{2,1,0:T(8,128)S(1)}, f32[1,136,128]{2,1,0:T(8,128)S(1)}, u32[]{:S(2)}, u32[]{:S(2)}) collective-permute-start(f32[1,136,128]{2,1,0:T(8,128)S(1)} %get-tuple-element.172), channel_id=1, source_target_pairs={{0,28},{4,0},{8,4},{12,8},{16,12},{20,16},{24,20},{28,24},{1,29},{... | collective-permute-start | bytes 208904 | tf_op jit(solution)/shard_map/ppermute | solution.py:175
  42.5 4.2 %collective-permute-done.4 = f32[1,136,128]{2,1,0:T(8,128)S(1)} collective-permute-done((f32[1,136,128]{2,1,0:T(8,128)S(1)}, f32[1,136,128]{2,1,0:T(8,128)S(1)}, u32[]{:S(2)}, u32[]{:S(2)}) %collective-permute-start.4) | collective-permute-done | bytes 69664 | tf_op jit(solution)/shard_map/ppermute | solution.py:175
  46.7 0.4 collective-permute-done.6
  47.1 0.6 gather_fusion
  48.1 5.0 %all-to-all-done = f32[8,128,128]{2,1,0:T(8,128)S(1)} async-done(((f32[8,128,128]{2,1,0:T(8,128)}), f32[8,128,128]{2,1,0:T(8,128)S(1)}, u32[]{:S(2)}, u32[]{:S(2)}) %all-to-all-start) | async-done | bytes 524320 | tf_op jit(solution)/shard_map/all_to_all | solution.py:184
  53.0 0.2 bitcast_multiply_fusion
  53.3 19.2 %while.16 = (s32[]{:T(128)}, f32[2,128,512]{1,2,0:T(8,128)S(1)}, f32[8,16,2,8,128]{4,3,2,1,0:T(8,128)S(1)}, s32[8,16,2]{1,0,2:T(8,128)S(1)}, s32[]{:T(128)}, /*index=5*/s32[]{:T(128)}) while((s32[]{:T(128)}, f32[2,128,512]{1,2,0:T(8,128)S(1)}, f32[8,16,2,8,128]{4,3,2,1,0:T(8,128)S(1)}, s32[8,16,2]{1,0,2:T(8,128)S(1)}, ...), condition=%wide.region_10.11_spmd.clone.clone, body=%wide.region_9.10_spmd.clone.clone.sunk | while | flops 403982464 | bytes 2279127 | solution.py:131
  53.4 1.5 %fusion.78 = f32[16,2,8,512]{3,2,1,0:T(8,128)S(1)} fusion(s32[16,128]{1,0:T(8,128)S(1)} %iota_add_fusion.4, f32[8,16,2,8,128]{4,3,2,1,0:T(8,128)S(1)} %get-tuple-element.239, s32[]{:T(128)} %get-tuple-element.231), kind=kOutput, calls=%fused_computation.6.clone.1 | convolution fusion | flops 202375168 | bytes 663556 | tf_op jit(solution)/shard_map/while/body/eval_jaxpr/vmwn,vny->vmwy/dot_general | solution.py:121
  54.9 0.1 fusion.79
  55.0 0.7 fusion.80
  55.8 1.5 %fusion.78 = f32[16,2,8,512]{3,2,1,0:T(8,128)S(1)} fusion(s32[16,128]{1,0:T(8,128)S(1)} %iota_add_fusion.4, f32[8,16,2,8,128]{4,3,2,1,0:T(8,128)S(1)} %get-tuple-element.239, s32[]{:T(128)} %get-tuple-element.231), kind=kOutput, calls=%fused_computation.6.clone.1 | convolution fusion | flops 202375168 | bytes 663556 | tf_op jit(solution)/shard_map/while/body/eval_jaxpr/vmwn,vny->vmwy/dot_general | solution.py:121
  57.3 0.1 fusion.79
  57.4 0.7 fusion.80
  58.2 1.5 %fusion.78 = f32[16,2,8,512]{3,2,1,0:T(8,128)S(1)} fusion(s32[16,128]{1,0:T(8,128)S(1)} %iota_add_fusion.4, f32[8,16,2,8,128]{4,3,2,1,0:T(8,128)S(1)} %get-tuple-element.239, s32[]{:T(128)} %get-tuple-element.231), kind=kOutput, calls=%fused_computation.6.clone.1 | convolution fusion | flops 202375168 | bytes 663556 | tf_op jit(solution)/shard_map/while/body/eval_jaxpr/vmwn,vny->vmwy/dot_general | solution.py:121
  59.7 0.1 fusion.79
  59.8 0.7 fusion.80
  60.6 1.5 %fusion.78 = f32[16,2,8,512]{3,2,1,0:T(8,128)S(1)} fusion(s32[16,128]{1,0:T(8,128)S(1)} %iota_add_fusion.4, f32[8,16,2,8,128]{4,3,2,1,0:T(8,128)S(1)} %get-tuple-element.239, s32[]{:T(128)} %get-tuple-element.231), kind=kOutput, calls=%fused_computation.6.clone.1 | convolution fusion | flops 202375168 | bytes 663556 | tf_op jit(solution)/shard_map/while/body/eval_jaxpr/vmwn,vny->vmwy/dot_general | solution.py:121
  62.1 0.1 fusion.79
  62.2 0.7 fusion.80
  63.0 1.5 %fusion.78 = f32[16,2,8,512]{3,2,1,0:T(8,128)S(1)} fusion(s32[16,128]{1,0:T(8,128)S(1)} %iota_add_fusion.4, f32[8,16,2,8,128]{4,3,2,1,0:T(8,128)S(1)} %get-tuple-element.239, s32[]{:T(128)} %get-tuple-element.231), kind=kOutput, calls=%fused_computation.6.clone.1 | convolution fusion | flops 202375168 | bytes 663556 | tf_op jit(solution)/shard_map/while/body/eval_jaxpr/vmwn,vny->vmwy/dot_general | solution.py:121
  64.5 0.1 fusion.79
  64.6 0.7 fusion.80
  65.5 1.5 %fusion.78 = f32[16,2,8,512]{3,2,1,0:T(8,128)S(1)} fusion(s32[16,128]{1,0:T(8,128)S(1)} %iota_add_fusion.4, f32[8,16,2,8,128]{4,3,2,1,0:T(8,128)S(1)} %get-tuple-element.239, s32[]{:T(128)} %get-tuple-element.231), kind=kOutput, calls=%fused_computation.6.clone.1 | convolution fusion | flops 202375168 | bytes 663556 | tf_op jit(solution)/shard_map/while/body/eval_jaxpr/vmwn,vny->vmwy/dot_general | solution.py:121
  66.9 0.1 fusion.79
  67.0 0.7 fusion.80
  67.9 1.5 %fusion.78 = f32[16,2,8,512]{3,2,1,0:T(8,128)S(1)} fusion(s32[16,128]{1,0:T(8,128)S(1)} %iota_add_fusion.4, f32[8,16,2,8,128]{4,3,2,1,0:T(8,128)S(1)} %get-tuple-element.239, s32[]{:T(128)} %get-tuple-element.231), kind=kOutput, calls=%fused_computation.6.clone.1 | convolution fusion | flops 202375168 | bytes 663556 | tf_op jit(solution)/shard_map/while/body/eval_jaxpr/vmwn,vny->vmwy/dot_general | solution.py:121
  69.3 0.1 fusion.79
  69.4 0.7 fusion.80
  70.3 1.5 %fusion.78 = f32[16,2,8,512]{3,2,1,0:T(8,128)S(1)} fusion(s32[16,128]{1,0:T(8,128)S(1)} %iota_add_fusion.4, f32[8,16,2,8,128]{4,3,2,1,0:T(8,128)S(1)} %get-tuple-element.239, s32[]{:T(128)} %get-tuple-element.231), kind=kOutput, calls=%fused_computation.6.clone.1 | convolution fusion | flops 202375168 | bytes 663556 | tf_op jit(solution)/shard_map/while/body/eval_jaxpr/vmwn,vny->vmwy/dot_general | solution.py:121
  71.7 0.1 fusion.79
  71.8 0.7 fusion.80
  72.6 0.2 copy.79
  72.8 0.8 %slice_divide_fusion = (f32[1,128,512]{2,1,0:T(8,128)}, f32[1,128,512]{2,1,0:T(8,128)}) fusion(f32[2,128,512]{2,1,0:T(8,128)S(1)} %copy.79), kind=kLoop, calls=%fused_computation.54 | loop fusion | flops 131072 | bytes 1048576 | tf_op jit(solution)/shard_map/div | solution.py:200
  (87 shorter events, 1.9 us)
Async XLA Ops:
  14.0 2.3 %copy-start = (s32[2,256,128]{2,1,0:T(8,128)S(1)}, s32[2,256,128]{2,1,0:T(8,128)}, u32[]{:S(2)}) copy-start(s32[2,256,128]{2,1,0:T(8,128)} %param.20) | copy-start | bytes 786436
  14.0 3.7 %copy-start.2 = (s32[64,1]{0,1:T(1,128)S(1)}, s32[64,1]{0,1:T(1,128)}, u32[]{:S(2)}) copy-start(s32[64,1]{0,1:T(1,128)} %param.23) | copy-start | bytes 772
  14.0 3.8 %copy-start.1 = (s32[2,1]{0,1:T(1,128)S(1)}, s32[2,1]{0,1:T(1,128)}, u32[]{:S(2)}) copy-start(s32[2,1]{0,1:T(1,128)} %param.22) | copy-start | bytes 28
  20.0 26.7 %collective-permute-start.5 = (f32[1,136,128]{2,1,0:T(8,128)S(1)}, f32[1,136,128]{2,1,0:T(8,128)S(1)}, u32[]{:S(2)}, u32[]{:S(2)}) collective-permute-start(f32[1,136,128]{2,1,0:T(8,128)S(1)} %fusion.41), channel_id=1, source_target_pairs={{0,24},{4,28},{8,0},{12,4},{16,8},{20,12},{24,16},{28,20},{1,25},{... | collective-permute-start | bytes 208904 | tf_op jit(solution)/shard_map/ppermute | solution.py:175
  25.1 11.9 %collective-permute-start = (f32[1,136,128]{2,1,0:T(8,128)S(1)}, f32[1,136,128]{2,1,0:T(8,128)S(1)}, u32[]{:S(2)}, u32[]{:S(2)}) collective-permute-start(f32[1,136,128]{2,1,0:T(8,128)S(1)} %get-tuple-element.173), channel_id=1, source_target_pairs={{0,4},{4,8},{8,12},{12,16},{16,20},{20,24},{24,28},{28,0},{1,5},{5... | collective-permute-start | bytes 208904 | tf_op jit(solution)/shard_map/ppermute | solution.py:175
  26.7 14.2 %collective-permute-start.1 = (f32[1,136,128]{2,1,0:T(8,128)S(1)}, f32[1,136,128]{2,1,0:T(8,128)S(1)}, u32[]{:S(2)}, u32[]{:S(2)}) collective-permute-start(f32[1,136,128]{2,1,0:T(8,128)S(1)} %get-tuple-element.174), channel_id=1, source_target_pairs={{0,8},{4,12},{8,16},{12,20},{16,24},{20,28},{24,0},{28,4},{1,9},{5... | collective-permute-start | bytes 208904 | tf_op jit(solution)/shard_map/ppermute | solution.py:175
  26.7 15.7 %collective-permute-start.2 = (f32[1,136,128]{2,1,0:T(8,128)S(1)}, f32[1,136,128]{2,1,0:T(8,128)S(1)}, u32[]{:S(2)}, u32[]{:S(2)}) collective-permute-start(f32[1,136,128]{2,1,0:T(8,128)S(1)} %get-tuple-element.175), channel_id=1, source_target_pairs={{0,12},{4,16},{8,20},{12,24},{16,28},{20,0},{24,4},{28,8},{1,13},{... | collective-permute-start | bytes 208904 | tf_op jit(solution)/shard_map/ppermute | solution.py:175
  27.7 14.8 %collective-permute-start.3 = (f32[1,136,128]{2,1,0:T(8,128)S(1)}, f32[1,136,128]{2,1,0:T(8,128)S(1)}, u32[]{:S(2)}, u32[]{:S(2)}) collective-permute-start(f32[1,136,128]{2,1,0:T(8,128)S(1)} %get-tuple-element.176), channel_id=1, source_target_pairs={{0,16},{4,20},{8,24},{12,28},{16,0},{20,4},{24,8},{28,12},{1,17},{... | collective-permute-start | bytes 208904 | tf_op jit(solution)/shard_map/ppermute | solution.py:175
  31.9 21.1 %all-to-all-start = ((f32[8,128,128]{2,1,0:T(8,128)}), f32[8,128,128]{2,1,0:T(8,128)S(1)}, u32[]{:S(2)}, u32[]{:S(2)}) async-start(f32[8,128,128]{2,1,0:T(8,128)} %reshape.397), calls=%async_computation | async-start | bytes 1048576 | tf_op jit(solution)/shard_map/all_to_all | solution.py:184
  37.0 9.7 %collective-permute-start.4 = (f32[1,136,128]{2,1,0:T(8,128)S(1)}, f32[1,136,128]{2,1,0:T(8,128)S(1)}, u32[]{:S(2)}, u32[]{:S(2)}) collective-permute-start(f32[1,136,128]{2,1,0:T(8,128)S(1)} %get-tuple-element.177), channel_id=1, source_target_pairs={{0,20},{4,24},{8,28},{12,0},{16,4},{20,8},{24,12},{28,16},{1,21},{... | collective-permute-start | bytes 208904 | tf_op jit(solution)/shard_map/ppermute | solution.py:175
  40.9 6.2 %collective-permute-start.6 = (f32[1,136,128]{2,1,0:T(8,128)S(1)}, f32[1,136,128]{2,1,0:T(8,128)S(1)}, u32[]{:S(2)}, u32[]{:S(2)}) collective-permute-start(f32[1,136,128]{2,1,0:T(8,128)S(1)} %get-tuple-element.172), channel_id=1, source_target_pairs={{0,28},{4,0},{8,4},{12,8},{16,12},{20,16},{24,20},{28,24},{1,29},{... | collective-permute-start | bytes 208904 | tf_op jit(solution)/shard_map/ppermute | solution.py:175
